TPU v7x, 32 devices: a whole 2x2x4 slice. The times are simulated.
32 devices in a mesh: tok: 4 (over y, x), feat: 8 (over z, core).
Axes of the slice: x: 2, y: 2, z: 4, core: 2. Of those that a mesh axis runs over, the one named last changes fastest.
Arguments:
- acts: bfloat16 [512, 8192], P('tok', 'feat'), may hold values from -6 to 6
- grad_out: bfloat16 [512, 28672], P('tok', 'feat'), may hold values from -6 to 6
- weight: bfloat16 [8192, 28672], P('tok', 'feat'), may hold values from -0.03125 to 0.03125
- block_rows: int32 [1024], P('feat'), may hold values from 0 to 63
- block_cols: int32 [1024], P('feat'), may hold values from 0 to 27
- block_count: int32 [8], P('feat'), may hold values from 1 to 128, as said below
Outputs:
- grad_in: bfloat16 [512, 8192], P('feat', 'tok')
- block_grads: bfloat16 [1024, 128, 128], P('feat', 'tok')
Inputs may be any that keep to these rules, and one draw needn't show every extreme that they name: `block_count`: each feat shard lists at most 128 blocks; one shard lists exactly 128; listed blocks of a shard may repeat.
All inputs are finite; a program needn't handle non-finite values.
Results may differ from a plain program's by a relative error of at most 0.001.
Values may be sent and summed in bfloat16 or wider, within the bound.
No kernel may reach another device: no remote copies, remote signals or barrier semaphores. Data moves between devices by JAX's collectives and lax.ppermute only.
A program may use at most 128 MiB of HBM per device.

v0:
```python
import jax
import jax.numpy as jnp
from jax import lax
from jax.sharding import PartitionSpec as P

BLK = 128


def per_device(acts, grad_out, weight, block_rows, block_cols, block_count):
    tok_dev = acts.shape[0]
    slot_count = block_rows.shape[0]
    active = (jnp.arange(slot_count, dtype=jnp.int32) < block_count[0]).astype(jnp.float32)
    full_acts = lax.all_gather(acts, "feat", axis=1, tiled=True)
    row_blocks = full_acts.shape[1] // BLK
    partial_sums = lax.dot_general(
        lax.all_gather(grad_out, "tok", axis=0, tiled=True),
        weight,
        (((1,), (1,)), ((), ())),
        preferred_element_type=jnp.float32,
    )
    act_sel = jnp.take(full_acts.reshape(tok_dev, row_blocks, BLK), block_rows, axis=1)
    grad_sel = jnp.take(grad_out.reshape(tok_dev, -1, BLK), block_cols, axis=1)
    partial_tiles = jnp.einsum(
        "tsa,tsb->sab", act_sel, grad_sel, preferred_element_type=jnp.float32
    )
    partial_tiles = partial_tiles * active[:, None, None]
    block_grads = lax.psum_scatter(partial_tiles, "tok", scatter_dimension=1, tiled=True).astype(
        jnp.bfloat16
    )
    grad_in = lax.psum_scatter(partial_sums, "feat", scatter_dimension=0, tiled=True).astype(
        jnp.bfloat16
    )
    return (grad_in, block_grads)


def solution(mesh):
    in_specs = (
        P("tok", "feat"),
        P("tok", "feat"),
        P("tok", "feat"),
        P("feat"),
        P("feat"),
        P("feat"),
    )
    out_specs = (P("feat", "tok"), P("feat", "tok", None))
    return jax.shard_map(
        per_device, mesh=mesh, in_specs=in_specs, out_specs=out_specs, check_vma=False
    )
```

profile of v0, /device:TPU:0, one launch (start us, length us, event | category | flops | bytes accessed | tf_op | source)
XLA Modules:
  0.0 240.9 jit_solution(17467459685259097102)
XLA Ops:
  7.2 0.0 all-gather.3.cloned.1.call-start
  7.2 0.7 all-gather.3.cloned.1.call-update
  7.9 0.0 all-gather.5.cloned.1.call-start
  7.9 1.8 copy.12
  9.7 0.0 all-gather.5.cloned.1.call-update
  9.8 0.0 reduce-scatter.3.cloned.1.call-start
  9.8 51.1 %all-gather.3.cloned.1.call-done = bf16[512,3584]{1,0:T(8,128)(2,1)} async-done(((bf16[128,3584]{1,0:T(8,128)(2,1)}), bf16[512,3584]{1,0:T(8,128)(2,1)}) %all-gather.3.cloned.1.call-update) | async-done | bytes 3670032 | tf_op jit(solution)/shard_map/all_gather | solution.py:16
  60.9 13.5 %fusion.13 = f32[512,2048]{1,0:T(8,128)} fusion(bf16[512,3584]{1,0:T(8,128)(2,1)} %all-gather.3.cloned.1.call-done, bf16[2048,3584]{1,0:T(8,128)(2,1)} %param.8), kind=kOutput, calls=%fused_computation.19 | convolution fusion | flops 7516192768 | bytes 22544384 | tf_op jit(solution)/shard_map/dot_general | solution.py:15
  74.4 0.0 reduce-scatter.3.cloned.1.call-update
  74.5 0.0 reduce-scatter.5.cloned.1.call-start
  74.5 1.1 copy-done
  75.6 0.6 copy.14
  76.9 0.6 copy.15
  77.6 0.0 copy-start.2
  77.6 3.0 %gather_fusion.1 = bf16[128,128,128]{2,1,0:T(8,128)(2,1)} fusion(bf16[128,28,128]{2,0,1:T(8,128)(2,1)S(1)} %copy.15, s32[1024]{0:T(1024)S(1)} %pad_clamp_fusion), kind=kCustom, calls=%fused_computation.1 | custom fusion | bytes 8389120 | tf_op jit(solution)/shard_map/jit(_take)/gather | solution.py:22
  80.7 11.6 %all-gather.5.cloned.1.call-done = bf16[128,8192]{0,1:T(8,128)(2,1)} async-done(((bf16[128,1024]{0,1:T(8,128)(2,1)}), bf16[128,8192]{0,1:T(8,128)(2,1)}) %all-gather.5.cloned.1.call-update) | async-done | bytes 2097168 | tf_op jit(solution)/shard_map/all_gather | solution.py:13
  92.2 3.2 %copy.13 = bf16[128,64,128]{2,0,1:T(8,128)(2,1)S(1)} copy(bf16[128,64,128]{0,2,1:T(8,128)(2,1)} %bitcast.17) | data formatting | bytes 4194304 | tf_op jit(solution)/shard_map/reshape | solution.py:21
  95.4 3.0 %gather_fusion = bf16[128,128,128]{2,1,0:T(8,128)(2,1)} fusion(bf16[128,64,128]{2,0,1:T(8,128)(2,1)S(1)} %copy.13, s32[1024]{0:T(1024)S(1)} %pad_clamp_fusion.1), kind=kCustom, calls=%fused_computation | custom fusion | bytes 8389120 | tf_op jit(solution)/shard_map/jit(_take)/gather | solution.py:21
  98.5 9.4 %broadcast_multiply_fusion = f32[128,128,128]{2,1,0:T(8,128)} fusion(f32[128]{0:T(128)S(1)} %get-tuple-element.2, bf16[128,128,128]{2,1,0:T(8,128)(2,1)} %gather_fusion.1, pred[128]{0:T(512)(128)(4,1)S(1)} %get-tuple-element.3, bf16[128,128,128]{2,1,0:T(8,128)(2,1)} %gather_fusion, pred[128]{0:T(512)(128)(4,1)S(1)} %compare_and_fusion.1), kind=kOutput, calls=%fused_computation.7 | convolution fusion | flops 543162368 | bytes 16777984 | tf_op jit(solution)/shard_map/tsa,tsb->sab/dot_general | solution.py:23
  107.9 0.0 reduce-scatter.5.cloned.1.call-update
  107.9 36.2 %reduce-scatter.3.cloned.1.call-done = f32[64,2048]{1,0:T(8,128)} async-done(((f32[512,2048]{1,0:T(8,128)}), f32[64,2048]{1,0:T(8,128)}) %reduce-scatter.3.cloned.1.call-update) | async-done | bytes 524304 | tf_op jit(solution)/shard_map/reduce_scatter | solution.py:30
  144.1 1.8 convert_element_type.13
  145.8 85.7 %reduce-scatter.5.cloned.1.call-done = f32[128,32,128]{2,1,0:T(8,128)} async-done(((f32[128,128,128]{2,1,0:T(8,128)}), f32[128,32,128]{2,1,0:T(8,128)}) %reduce-scatter.5.cloned.1.call-update) | async-done | bytes 2097168 | tf_op jit(solution)/shard_map/reduce_scatter | solution.py:27
  231.6 2.8 %convert_element_type.15 = bf16[128,32,128]{2,1,0:T(8,128)(2,1)} convert(f32[128,32,128]{2,1,0:T(8,128)} %reduce-scatter.5.cloned.1.call-done) | non-fusion elementwise | flops 524288 | bytes 3145728 | tf_op jit(solution)/shard_map/convert_element_type | solution.py:27
  (10 shorter events, 0.0 us)
Async XLA Ops:
  7.2 53.8 %all-gather.3.cloned.1.call-start = ((), (), s32[]{:S(2)}) async-start(), calls=%async_computation.2 | async-start | bytes 4587520 | tf_op jit(solution)/shard_map/all_gather | solution.py:16
  7.9 84.3 %all-gather.5.cloned.1.call-start = ((), (), s32[]{:S(2)}) async-start(), calls=%async_computation.4 | async-start | bytes 2359296 | tf_op jit(solution)/shard_map/all_gather | solution.py:13
  9.8 134.3 %reduce-scatter.3.cloned.1.call-start = ((), (), s32[]{:S(2)}) async-start(), calls=%async_computation.3 | async-start | bytes 4718592 | tf_op jit(solution)/shard_map/reduce_scatter | solution.py:30
  74.4 1.2 copy-start
  74.4 3.1 %copy-start.1 = (s32[128]{0:T(128)S(1)}, s32[128]{0:T(128)}, u32[]{:S(2)}) copy-start(s32[128]{0:T(128)} %param.10) | copy-start | bytes 1540
  74.5 157.1 %reduce-scatter.5.cloned.1.call-start = ((), (), s32[]{:S(2)}) async-start(), calls=%async_computation.5 | async-start | bytes 10485760 | tf_op jit(solution)/shard_map/reduce_scatter | solution.py:27
  77.6 3.0 %copy-start.2 = (s32[128]{0:T(128)S(1)}, s32[128]{0:T(128)}, u32[]{:S(2)}) copy-start(s32[128]{0:T(128)} %param.9) | copy-start | bytes 1540
Sparse Core Ops, SparseCore 0:
  9.8 51.0 all-gather.2
  63.1 29.0 all-gather.4
  94.5 49.4 reduce-scatter.2
  147.0 84.5 reduce-scatter.4
where the time goes:
time: 241 us
  waiting for transfers between devices  185 us (77%)
  matrix products  22.9 us (10%)
  between operations  14.5 us (6%)
  local copies, waits for them, and re-layouts  13.4 us (6%)
  other arithmetic  4.59 us (2%)
    reduce_scatter x1, waiting for transfers between devices, per_device(): lax.psum_scatter(partial_tiles, 'tok', scatter_dimension=1, tiled=True)  85.7 us
    all_gather x1, waiting for transfers between devices, per_device(): lax.all_gather(grad_out, 'tok', axis=0, tiled=True)  51.1 us
    reduce_scatter x1, waiting for transfers between devices, per_device(): lax.psum_scatter(partial_sums, 'feat', scatter_dimension=0, tiled=True)  36.2 us
    dot_general x1, matrix products, per_device(): lax.dot_general(lax.all_gather(grad_out, 'tok', axis=0, tiled=True), weig...  13.5 us
    all_gather x1, waiting for transfers between devices, per_device(): full_acts = lax.all_gather(acts, 'feat', axis=1, tiled=True)  11.6 us
    dot_general x1, matrix products, per_device(): jnp.einsum('tsa,tsb->sab', act_sel, grad_sel, preferred_element_type=jnp....  9.38 us
  transfers between devices with their start and end apart: 4, of which 4 were waited for; matrix products, arithmetic and copies ran while one was open for 15% of the time, Pallas kernels for 0%

commit v1 on v0

--- a/solution.py
+++ b/solution.py
@@ -10,7 +10,12 @@
     tok_dev = acts.shape[0]
     slot_count = block_rows.shape[0]
     active = (jnp.arange(slot_count, dtype=jnp.int32) < block_count[0]).astype(jnp.float32)
-    full_acts = lax.all_gather(acts, "feat", axis=1, tiled=True)
+    ring = [acts]
+    for hop in range(7):
+        ring.append(lax.ppermute(ring[-1], "feat", [(dev, (dev + 1) % 8) for dev in range(8)]))
+    full_acts = jnp.roll(
+        jnp.concatenate(ring[::-1], axis=1), (lax.axis_index("feat") + 1) * ring[0].shape[1], axis=1
+    )
     row_blocks = full_acts.shape[1] // BLK
     partial_sums = lax.dot_general(
         lax.all_gather(grad_out, "tok", axis=0, tiled=True),

time: 241 us -> 266 us (1.10)
  waiting for transfers between devices: 185 us -> 207 us
  local copies, waits for them, and re-layouts: 13.4 us -> 17.4 us
    ppermute x0 -> x7, waiting for transfers between devices: none -> 69.9 us  [per_device(): lax.ppermute(ring[-1], 'feat', [(dev, (dev + 1) % 8) for dev in range(8)])]
    reduce_scatter x1, waiting for transfers between devices: 36.2 us -> 0.02 us  [per_device(): lax.psum_scatter(partial_sums, 'feat', scatter_dimension=0, tiled=True)]
    all_gather x1 -> x0, waiting for transfers between devices: 11.6 us -> none  [per_device(): full_acts = lax.all_gather(acts, 'feat', axis=1, tiled=True)]
    reduce_scatter x1, waiting for transfers between devices: 85.7 us -> 83 us  [per_device(): lax.psum_scatter(partial_tiles, 'tok', scatter_dimension=1, tiled=True)]
    unnamed x8 -> x25, local copies, waits for them, and re-layouts: 3.52 us -> 5.98 us
  transfers between devices with their start and end apart: 4 -> 10, of which waited for: 4 -> 9; matrix products, arithmetic and copies ran while one was open for 15% -> 10% of each run, Pallas kernels for 0% -> 0%
where the time goes in v1:
time: 266 us
  waiting for transfers between devices  207 us (78%)
  matrix products  22.5 us (8%)
  local copies, waits for them, and re-layouts  17.4 us (7%)
  between operations  14.6 us (5%)
  other arithmetic  4.58 us (2%)
    reduce_scatter x1, waiting for transfers between devices, per_device(): lax.psum_scatter(partial_tiles, 'tok', scatter_dimension=1, tiled=True)  83 us
    ppermute x7, waiting for transfers between devices, per_device(): lax.ppermute(ring[-1], 'feat', [(dev, (dev + 1) % 8) for dev in range(8)])  69.9 us
    all_gather x1, waiting for transfers between devices, per_device(): lax.all_gather(grad_out, 'tok', axis=0, tiled=True)  53 us
    dot_general x1, matrix products, per_device(): lax.dot_general(lax.all_gather(grad_out, 'tok', axis=0, tiled=True), weig...  13.5 us
    dot_general x1, matrix products, per_device(): jnp.einsum('tsa,tsb->sab', act_sel, grad_sel, preferred_element_type=jnp....  8.99 us
    unnamed x25, local copies, waits for them, and re-layouts  5.98 us
  transfers between devices with their start and end apart: 10, of which 9 were waited for; matrix products, arithmetic and copies ran while one was open for 10% of the time, Pallas kernels for 0%

profile of v1, /device:TPU:0, one launch (start us, length us, event | category | flops | bytes accessed | tf_op | source)
XLA Modules:
  0.0 265.9 jit_solution(7186139740724737192)
XLA Ops:
  7.2 0.7 all-gather.2.cloned.1.call-update
  7.9 53.0 %all-gather.2.cloned.1.call-done = bf16[512,3584]{1,0:T(8,128)(2,1)} async-done(((bf16[128,3584]{1,0:T(8,128)(2,1)}), bf16[512,3584]{1,0:T(8,128)(2,1)}) %all-gather.2.cloned.1.call-update) | async-done | bytes 3670032 | tf_op jit(solution)/shard_map/all_gather | solution.py:21
  60.9 13.5 %fusion.13 = f32[512,2048]{1,0:T(8,128)} fusion(bf16[512,3584]{1,0:T(8,128)(2,1)} %all-gather.2.cloned.1.call-done, bf16[2048,3584]{1,0:T(8,128)(2,1)} %param.8), kind=kOutput, calls=%fused_computation.36 | convolution fusion | flops 7516192768 | bytes 22544384 | tf_op jit(solution)/shard_map/dot_general | solution.py:20
  74.5 0.9 copy-done.1
  75.6 7.6 %collective-permute-done = bf16[128,1024]{0,1:T(8,128)(2,1)S(1)} collective-permute-done((bf16[128,1024]{0,1:T(8,128)(2,1)S(1)}, bf16[128,1024]{0,1:T(8,128)(2,1)S(1)}, u32[]{:S(2)}, u32[]{:S(2)}) %collective-permute-start) | collective-permute-done | bytes 262176 | tf_op jit(solution)/shard_map/ppermute | solution.py:15
  83.2 13.2 %collective-permute-done.1 = bf16[128,1024]{0,1:T(8,128)(2,1)S(1)} collective-permute-done((bf16[128,1024]{0,1:T(8,128)(2,1)S(1)}, bf16[128,1024]{0,1:T(8,128)(2,1)S(1)}, u32[]{:S(2)}, u32[]{:S(2)}) %collective-permute-start.1) | collective-permute-done | bytes 262176 | tf_op jit(solution)/shard_map/ppermute | solution.py:15
  96.4 13.4 %collective-permute-done.2 = bf16[128,1024]{0,1:T(8,128)(2,1)S(1)} collective-permute-done((bf16[128,1024]{0,1:T(8,128)(2,1)S(1)}, bf16[128,1024]{0,1:T(8,128)(2,1)S(1)}, u32[]{:S(2)}, u32[]{:S(2)}) %collective-permute-start.2) | collective-permute-done | bytes 262176 | tf_op jit(solution)/shard_map/ppermute | solution.py:15
  109.8 13.4 %collective-permute-done.3 = bf16[128,1024]{0,1:T(8,128)(2,1)S(1)} collective-permute-done((bf16[128,1024]{0,1:T(8,128)(2,1)S(1)}, bf16[128,1024]{0,1:T(8,128)(2,1)S(1)}, u32[]{:S(2)}, u32[]{:S(2)}) %collective-permute-start.3) | collective-permute-done | bytes 262176 | tf_op jit(solution)/shard_map/ppermute | solution.py:15
  123.2 11.8 %collective-permute-done.4 = bf16[128,1024]{0,1:T(8,128)(2,1)S(1)} collective-permute-done((bf16[128,1024]{0,1:T(8,128)(2,1)S(1)}, bf16[128,1024]{0,1:T(8,128)(2,1)S(1)}, u32[]{:S(2)}, u32[]{:S(2)}) %collective-permute-start.4) | collective-permute-done | bytes 262176 | tf_op jit(solution)/shard_map/ppermute | solution.py:15
  135.1 7.7 %collective-permute-done.5 = bf16[128,1024]{0,1:T(8,128)(2,1)} collective-permute-done((bf16[128,1024]{0,1:T(8,128)(2,1)S(1)}, bf16[128,1024]{0,1:T(8,128)(2,1)}, u32[]{:S(2)}, u32[]{:S(2)}) %collective-permute-start.5) | collective-permute-done | bytes 262176 | tf_op jit(solution)/shard_map/ppermute | solution.py:15
  143.4 0.6 copy.17
  144.7 3.0 %gather_fusion.1 = bf16[128,128,128]{2,1,0:T(8,128)(2,1)} fusion(bf16[128,28,128]{2,0,1:T(8,128)(2,1)S(1)} %copy.17, s32[1024]{0:T(1024)S(1)} %get-tuple-element.2), kind=kCustom, calls=%fused_computation.1 | custom fusion | bytes 8389120 | tf_op jit(solution)/shard_map/jit(_take)/gather | solution.py:27
  147.7 2.9 %collective-permute-done.6 = bf16[128,1024]{0,1:T(8,128)(2,1)} collective-permute-done((bf16[128,1024]{0,1:T(8,128)(2,1)}, bf16[128,1024]{0,1:T(8,128)(2,1)}, u32[]{:S(2)}, u32[]{:S(2)}) %collective-permute-start.6) | collective-permute-done | bytes 262176 | tf_op jit(solution)/shard_map/ppermute | solution.py:15
  150.6 1.0 constant_dynamic-update-slice_fusion.15
  151.6 1.0 constant_dynamic-update-slice_fusion.14
  152.9 1.0 constant_dynamic-update-slice_fusion.7
  153.8 1.0 constant_dynamic-update-slice_fusion.6
  155.1 1.5 constant_dynamic-slice_fusion
  156.6 3.2 %copy.15 = bf16[128,64,128]{2,0,1:T(8,128)(2,1)S(1)} copy(bf16[128,64,128]{0,2,1:T(8,128)(2,1)} %bitcast.16) | data formatting | bytes 4194304 | tf_op jit(solution)/shard_map/reshape | solution.py:26
  159.8 3.0 %gather_fusion = bf16[128,128,128]{2,1,0:T(8,128)(2,1)} fusion(bf16[128,64,128]{2,0,1:T(8,128)(2,1)S(1)} %copy.15, s32[1024]{0:T(1024)S(1)} %get-tuple-element.3), kind=kCustom, calls=%fused_computation | custom fusion | bytes 8389120 | tf_op jit(solution)/shard_map/jit(_take)/gather | solution.py:26
  162.8 9.0 %broadcast_multiply_fusion = f32[128,128,128]{2,1,0:T(8,128)} fusion(f32[128]{0:T(128)S(1)} %get-tuple-element.4, bf16[128,128,128]{2,1,0:T(8,128)(2,1)} %gather_fusion.1, pred[128]{0:T(512)(128)(4,1)S(1)} %get-tuple-element.5, bf16[128,128,128]{2,1,0:T(8,128)(2,1)} %gather_fusion, pred[128]{0:T(512)(128)(4,1)S(1)} %compare_and_fusion.1), kind=kOutput, calls=%fused_computation.7 | convolution fusion | flops 543162368 | bytes 16777984 | tf_op jit(solution)/shard_map/tsa,tsb->sab/dot_general | solution.py:28
  171.9 1.8 convert_element_type.13
  173.7 83.0 %reduce-scatter.5.cloned.1.call-done = f32[128,32,128]{2,1,0:T(8,128)} async-done(((f32[128,128,128]{2,1,0:T(8,128)}), f32[128,32,128]{2,1,0:T(8,128)}) %reduce-scatter.5.cloned.1.call-update) | async-done | bytes 2097168 | tf_op jit(solution)/shard_map/reduce_scatter | solution.py:32
  256.6 2.8 %convert_element_type.15 = bf16[128,32,128]{2,1,0:T(8,128)(2,1)} convert(f32[128,32,128]{2,1,0:T(8,128)} %reduce-scatter.5.cloned.1.call-done) | non-fusion elementwise | flops 524288 | bytes 3145728 | tf_op jit(solution)/shard_map/convert_element_type | solution.py:32
  (39 shorter events, 1.5 us)
Async XLA Ops:
  7.2 53.8 %all-gather.2.cloned.1.call-start = ((), (), s32[]{:S(2)}) async-start(), calls=%async_computation.2 | async-start | bytes 4587520 | tf_op jit(solution)/shard_map/all_gather | solution.py:21
  7.9 164.0 %reduce-scatter.3.cloned.1.call-start = ((), (), s32[]{:S(2)}) async-start(), calls=%async_computation.3 | async-start | bytes 4718592 | tf_op jit(solution)/shard_map/reduce_scatter | solution.py:35
  74.5 0.9 copy-start.1
  74.5 48.7 %copy-start.3 = (s32[128]{0:T(128)S(1)}, s32[128]{0:T(128)}, u32[]{:S(2)}) copy-start(s32[128]{0:T(128)} %param.9) | copy-start | bytes 1540
  74.5 60.6 %copy-start.2 = (s32[128]{0:T(128)S(1)}, s32[128]{0:T(128)}, u32[]{:S(2)}) copy-start(s32[128]{0:T(128)} %param.10) | copy-start | bytes 1540
  74.5 68.3 %copy-start = (bf16[128,3584]{1,0:T(8,128)(2,1)S(1)}, bf16[128,3584]{1,0:T(8,128)(2,1)}, u32[]{:S(2)}) copy-start(bf16[128,3584]{1,0:T(8,128)(2,1)} %param.7) | copy-start | bytes 2752516
  74.5 182.1 %reduce-scatter.5.cloned.1.call-start = ((), (), s32[]{:S(2)}) async-start(), calls=%async_computation.4 | async-start | bytes 10485760 | tf_op jit(solution)/shard_map/reduce_scatter | solution.py:32
  75.6 7.7 %collective-permute-start = (bf16[128,1024]{0,1:T(8,128)(2,1)S(1)}, bf16[128,1024]{0,1:T(8,128)(2,1)S(1)}, u32[]{:S(2)}, u32[]{:S(2)}) collective-permute-start(bf16[128,1024]{0,1:T(8,128)(2,1)S(1)} %copy.12), channel_id=1, source_target_pairs={{0,1},{1,2},{2,3},{3,4},{4,5},{5,6},{6,7},{7,0},{8,9},{9,10},{10,1... | collective-permute-start | bytes 786440 | tf_op jit(solution)/shard_map/ppermute | solution.py:15
  83.2 13.2 %collective-permute-start.1 = (bf16[128,1024]{0,1:T(8,128)(2,1)S(1)}, bf16[128,1024]{0,1:T(8,128)(2,1)S(1)}, u32[]{:S(2)}, u32[]{:S(2)}) collective-permute-start(bf16[128,1024]{0,1:T(8,128)(2,1)S(1)} %collective-permute-done), channel_id=1, source_target_pairs={{0,1},{1,2},{2,3},{3,4},{4,5},{5,6},{6,7},{7,0},{8,9},{9,10},{10,1... | collective-permute-start | bytes 786440 | tf_op jit(solution)/shard_map/ppermute | solution.py:15
  96.4 13.4 %collective-permute-start.2 = (bf16[128,1024]{0,1:T(8,128)(2,1)S(1)}, bf16[128,1024]{0,1:T(8,128)(2,1)S(1)}, u32[]{:S(2)}, u32[]{:S(2)}) collective-permute-start(bf16[128,1024]{0,1:T(8,128)(2,1)S(1)} %collective-permute-done.1), channel_id=1, source_target_pairs={{0,1},{1,2},{2,3},{3,4},{4,5},{5,6},{6,7},{7,0},{8,9},{9,10},{10,1... | collective-permute-start | bytes 786440 | tf_op jit(solution)/shard_map/ppermute | solution.py:15
  109.8 13.4 %collective-permute-start.3 = (bf16[128,1024]{0,1:T(8,128)(2,1)S(1)}, bf16[128,1024]{0,1:T(8,128)(2,1)S(1)}, u32[]{:S(2)}, u32[]{:S(2)}) collective-permute-start(bf16[128,1024]{0,1:T(8,128)(2,1)S(1)} %collective-permute-done.2), channel_id=1, source_target_pairs={{0,1},{1,2},{2,3},{3,4},{4,5},{5,6},{6,7},{7,0},{8,9},{9,10},{10,1... | collective-permute-start | bytes 786440 | tf_op jit(solution)/shard_map/ppermute | solution.py:15
  123.2 11.8 %collective-permute-start.4 = (bf16[128,1024]{0,1:T(8,128)(2,1)S(1)}, bf16[128,1024]{0,1:T(8,128)(2,1)S(1)}, u32[]{:S(2)}, u32[]{:S(2)}) collective-permute-start(bf16[128,1024]{0,1:T(8,128)(2,1)S(1)} %collective-permute-done.3), channel_id=1, source_target_pairs={{0,1},{1,2},{2,3},{3,4},{4,5},{5,6},{6,7},{7,0},{8,9},{9,10},{10,1... | collective-permute-start | bytes 786440 | tf_op jit(solution)/shard_map/ppermute | solution.py:15
  135.0 7.7 %collective-permute-start.5 = (bf16[128,1024]{0,1:T(8,128)(2,1)S(1)}, bf16[128,1024]{0,1:T(8,128)(2,1)}, u32[]{:S(2)}, u32[]{:S(2)}) collective-permute-start(bf16[128,1024]{0,1:T(8,128)(2,1)S(1)} %collective-permute-done.4), channel_id=1, source_target_pairs={{0,1},{1,2},{2,3},{3,4},{4,5},{5,6},{6,7},{7,0},{8,9},{9,10},{10,1... | collective-permute-start | bytes 786440 | tf_op jit(solution)/shard_map/ppermute | solution.py:15
  142.7 7.9 %collective-permute-start.6 = (bf16[128,1024]{0,1:T(8,128)(2,1)}, bf16[128,1024]{0,1:T(8,128)(2,1)}, u32[]{:S(2)}, u32[]{:S(2)}) collective-permute-start(bf16[128,1024]{0,1:T(8,128)(2,1)} %collective-permute-done.5), channel_id=1, source_target_pairs={{0,1},{1,2},{2,3},{3,4},{4,5},{5,6},{6,7},{7,0},{8,9},{9,10},{10,1... | collective-permute-start | bytes 786440 | tf_op jit(solution)/shard_map/ppermute | solution.py:15
Sparse Core Ops, SparseCore 0:
  9.8 51.0 all-gather.1
  74.6 60.3 reduce-scatter.2
  172.0 84.5 reduce-scatter.4
